TPU v7x, 32 devices: a whole 2x2x4 slice. The times are simulated.
32 devices in a mesh: row: 8 (over z, y), col: 4 (over x, core).
Axes of the slice: x: 2, y: 2, z: 4, core: 2. Of those that a mesh axis runs over, the one named last changes fastest.
Arguments:
- x_t: bfloat16 [128, 8192], P('col', 'row'), may hold values from -6 to 6
- tiles: bfloat16 [64, 128, 128], P('row'), may hold values from -0.375 to 0.375
- tile_owner: int32 [64, 1], P('row'), may hold values from 0 to 7; in each aligned block of 8 rows (0 to 7, 8 to 15, ...) at most 2 rows name the same one
- tile_local: int32 [64, 2], P('row'), may hold values from 0 to 7
- weight: bfloat16 [128, 256], replicated, may hold values from -0.5 to 0.5
- cotangent: bfloat16 [8192, 256], P('row'), may hold values from -0.0625 to 0.0625
Outputs:
- act: bfloat16 [8192, 256], P('row')
- grad_w: float32 [128, 256], P('col')
Inputs may be any that keep to these rules, and one draw needn't show every extreme that they name: `tile_owner`: within the 8 stored tiles of one index of row (aligned blocks of 8 rows) no owner appears more than 2 times, and some owner appears exactly 2 times.
All inputs are finite; a program needn't handle non-finite values.
Results may differ from a plain program's by a relative error of at most 0.0059.
Values may be sent and summed in bfloat16 or wider, within the bound.
No kernel may reach another device: no remote copies, remote signals or barrier semaphores. Data moves between devices by JAX's collectives and lax.ppermute only.
A program may use at most 64 MiB of HBM per device.

v0:
```python
import jax
import jax.numpy as jnp
from jax import lax
from jax.sharding import PartitionSpec as P


def body(x_t, tiles, tile_owner, tile_local, weight, cotangent):
    n_row = lax.axis_size("row")
    n_tiles, tile_dim = (tiles.shape[0], tiles.shape[1])
    feat_q, rows = x_t.shape
    n_blocks = rows // tile_dim
    capacity = 2 * (n_tiles // n_row)
    xb = x_t.reshape(feat_q, n_blocks, tile_dim).transpose(1, 0, 2)
    flat_blocks = xb.reshape(n_blocks, feat_q * tile_dim)
    owner = tile_owner[:, 0]
    row_local = tile_local[:, 0]
    col_local = tile_local[:, 1]
    owner_hot = (owner[:, None] == jnp.arange(n_row, dtype=jnp.int32)[None, :]).astype(jnp.int32)
    rank = jnp.sum(owner_hot * (jnp.cumsum(owner_hot, axis=0) - 1), axis=1)
    slot = owner * capacity + rank
    requests = (
        jnp.zeros((n_row * capacity,), jnp.int32).at[slot].set(col_local).reshape(n_row, capacity)
    )
    own_blocks = jnp.take(xb, row_local, axis=0)
    mirror_terms = jnp.einsum(
        "tfi,tij->tfj", own_blocks, tiles, preferred_element_type=jnp.float32
    ).astype(jnp.bfloat16)
    outgoing = jnp.zeros((n_row * capacity, feat_q * tile_dim), jnp.bfloat16)
    outgoing = (
        outgoing.at[slot]
        .set(mirror_terms.reshape(n_tiles, feat_q * tile_dim))
        .reshape(n_row, capacity, feat_q * tile_dim)
    )
    block_ids = lax.all_to_all(requests, "row", split_axis=0, concat_axis=0, tiled=True)
    picked = jnp.take(flat_blocks, block_ids, axis=0)
    fetched = lax.all_to_all(picked, "row", split_axis=0, concat_axis=0, tiled=True)
    incoming = lax.all_to_all(outgoing, "row", split_axis=0, concat_axis=0, tiled=True)
    fetched_tiles = jnp.take(fetched.reshape(n_row * capacity, feat_q, tile_dim), slot, axis=0)
    forward_terms = jnp.einsum(
        "tfj,tij->tfi", fetched_tiles, tiles, preferred_element_type=jnp.float32
    )
    block_range = jnp.arange(n_blocks, dtype=jnp.int32)
    row_hot = (row_local[:, None] == block_range[None, :]).astype(jnp.float32)
    local_sum = jnp.einsum("tfi,tb->fbi", forward_terms, row_hot, precision=lax.Precision.HIGHEST)
    in_hot = (block_ids.reshape(-1)[:, None] == block_range[None, :]).astype(jnp.bfloat16)
    mirror_sum = jnp.einsum(
        "sk,sb->bk",
        incoming.reshape(n_row * capacity, feat_q * tile_dim),
        in_hot,
        preferred_element_type=jnp.float32,
    )
    mirror_sum = mirror_sum.reshape(n_blocks, feat_q, tile_dim).transpose(1, 0, 2)
    z_part = (local_sum + mirror_sum).reshape(feat_q, rows).astype(jnp.bfloat16)
    w_rows = lax.dynamic_slice_in_dim(weight, lax.axis_index("col") * feat_q, feat_q, 0)
    partial_y = lax.dot_general(
        z_part, w_rows, (((0,), (0,)), ((), ())), preferred_element_type=jnp.float32
    )
    y_full = lax.psum(partial_y, "col")
    act = jax.nn.silu(y_full).astype(jnp.bfloat16)
    sig = jax.nn.sigmoid(y_full)
    grad_y = (cotangent.astype(jnp.float32) * sig * (1.0 + y_full * (1.0 - sig))).astype(
        jnp.bfloat16
    )
    grad_part = jnp.dot(z_part, grad_y, preferred_element_type=jnp.float32)
    grad_w = lax.psum(grad_part, "row")
    return (act, grad_w)


def solution(mesh):
    in_specs = (
        P("col", "row"),
        P("row", None, None),
        P("row", None),
        P("row", None),
        P(),
        P("row", None),
    )
    out_specs = (P("row", None), P("col", None))
    return jax.shard_map(body, mesh=mesh, in_specs=in_specs, out_specs=out_specs, check_vma=False)
```

profile of v0, /device:TPU:0, one launch (start us, length us, event | category | flops | bytes accessed | tf_op | source)
XLA Modules:
  0.0 130.2 jit_solution(15986856091040692897)
XLA Ops:
  7.2 0.0 copy-start
  7.2 0.8 fusion.37
  7.9 0.0 copy-start.2
  7.9 0.7 copy-done.2
  8.6 0.1 fusion.24
  8.7 0.2 select_reduce_fusion
  8.9 0.6 scatter_custom_fusion
  9.5 0.7 all_to_all.16
  10.2 0.0 copy-start.3
  10.2 7.4 %all-to-all-start = ((s32[8,1,2]{2,1,0:T(1,128)}), s32[8,1,2]{2,1,0:T(1,128)S(1)}, u32[]{:S(2)}, u32[]{:S(2)}) async-start(s32[8,1,2]{2,1,0:T(1,128)} %bitcast.7), calls=%async_computation | async-start | bytes 8192 | tf_op jit(solution)/shard_map/all_to_all | solution.py:34
  17.6 0.0 copy-done.3
  17.6 0.9 bitcast_bitcast_fusion.1
  18.5 0.6 gather_fusion.2
  19.0 0.0 copy-done
  19.1 0.2 fusion.1
  19.3 0.8 scatter_custom_fusion.1
  20.1 0.7 reshape.80
  20.8 3.1 %all-to-all-done = s32[8,1,2]{2,1,0:T(1,128)S(1)} async-done(((s32[8,1,2]{2,1,0:T(1,128)}), s32[8,1,2]{2,1,0:T(1,128)S(1)}, u32[]{:S(2)}, u32[]{:S(2)}) %all-to-all-start) | async-done | bytes 96 | tf_op jit(solution)/shard_map/all_to_all | solution.py:34
  24.0 3.4 %all-to-all-start.2 = ((bf16[8,2,4096]{2,1,0:T(2,128)(2,1)}), bf16[8,2,4096]{2,1,0:T(2,128)(2,1)S(1)}, u32[]{:S(2)}, u32[]{:S(2)}) async-start(bf16[8,2,4096]{2,1,0:T(2,128)(2,1)} %reshape.80), calls=%async_computation.2 | async-start | bytes 262144 | tf_op jit(solution)/shard_map/all_to_all | solution.py:37
  27.4 0.1 copy.33
  27.4 0.1 copy.34
  27.5 0.1 copy.37
  27.6 0.1 reshape.84
  27.7 0.6 gather_fusion
  28.4 0.1 reshape.83
  28.5 0.8 broadcast_select_fusion
  29.3 5.3 %all-to-all-done.2 = bf16[8,2,4096]{2,1,0:T(2,128)(2,1)S(1)} async-done(((bf16[8,2,4096]{2,1,0:T(2,128)(2,1)}), bf16[8,2,4096]{2,1,0:T(2,128)(2,1)S(1)}, u32[]{:S(2)}, u32[]{:S(2)}) %all-to-all-start.2) | async-done | bytes 131104 | tf_op jit(solution)/shard_map/all_to_all | solution.py:37
  34.6 3.4 %all-to-all-start.1 = ((bf16[8,2,4096]{2,1,0:T(2,128)(2,1)}), bf16[8,2,4096]{2,1,0:T(2,128)(2,1)S(1)}, u32[]{:S(2)}, u32[]{:S(2)}) async-start(bf16[8,2,4096]{2,1,0:T(2,128)(2,1)} %broadcast_select_fusion), calls=%async_computation.1 | async-start | bytes 262144 | tf_op jit(solution)/shard_map/all_to_all | solution.py:36
  38.0 0.0 all-reduce.2.cloned.1.call-start
  38.1 0.5 broadcast.107
  38.6 0.7 reduce.3
  39.3 0.1 eq.53
  39.3 0.1 reshape.81
  39.4 5.9 %all-to-all-done.1 = bf16[8,2,4096]{2,1,0:T(2,128)(2,1)S(1)} async-done(((bf16[8,2,4096]{2,1,0:T(2,128)(2,1)}), bf16[8,2,4096]{2,1,0:T(2,128)(2,1)S(1)}, u32[]{:S(2)}, u32[]{:S(2)}) %all-to-all-start.1) | async-done | bytes 131104 | tf_op jit(solution)/shard_map/all_to_all | solution.py:36
  45.3 0.1 reshape.78
  45.4 0.6 gather_fusion.1
  46.0 0.3 fusion.15
  46.3 0.3 fusion.5
  46.5 0.1 fusion
  46.7 2.1 %fusion.8 = f32[1024,256]{1,0:T(8,128)} fusion(bf16[4,8,8,128]{3,2,1,0:T(8,128)(2,1)S(1)} %bitcast.68, bf16[128,256]{1,0:T(8,128)(2,1)} %param.10, s32[]{:T(128)S(6)} %select_n.53), kind=kOutput, calls=%fused_computation.19 | convolution fusion | flops 16777216 | bytes 1130500 | tf_op jit(solution)/shard_map/dot_general | solution.py:55
  48.8 0.0 copy-start.4
  48.8 0.0 all-reduce.2.cloned.1.call-update
  48.8 34.0 %all-reduce.2.cloned.1.call-done = f32[1024,256]{1,0:T(8,128)} async-done(((f32[1024,256]{1,0:T(8,128)}), f32[1024,256]{1,0:T(8,128)}) %all-reduce.2.cloned.1.call-update) | async-done | bytes 1048592 | tf_op jit(solution)/shard_map/psum | solution.py:58
  82.8 0.0 copy-done.4
  82.8 1.8 %fusion.2 = f32[32,256]{1,0:T(8,128)S(1)} fusion(f32[1024,256]{1,0:T(8,128)} %all-reduce.2.cloned.1.call-done, bf16[1024,256]{1,0:T(8,128)(2,1)S(1)} %copy-done.4, bf16[4,8,8,128]{3,2,1,0:T(8,128)(2,1)S(1)} %bitcast.69), kind=kOutput, calls=%fused_computation.12 | convolution fusion | flops 19398656 | bytes 1671168 | tf_op jit(solution)/shard_map/dot_general | solution.py:64
  84.6 37.7 %psum.15 = f32[32,256]{1,0:T(8,128)} all-reduce(f32[32,256]{1,0:T(8,128)S(1)} %fusion.2), channel_id=1, replica_groups=mesh['row'=8,'col'=4] {'row'}, use_global_device_ids=true, to_apply=%region_5.6 | all-reduce | flops 8192 | bytes 65536 | tf_op jit(solution)/shard_map/psum | solution.py:65
  122.3 0.0 copy-done.1
  122.3 1.1 multiply_convert_fusion.1
  (10 shorter events, 0.1 us)
Async XLA Ops:
  7.2 11.9 %copy-start = (bf16[8,128,128]{2,1,0:T(8,128)(2,1)S(1)}, bf16[8,128,128]{2,1,0:T(8,128)(2,1)}, u32[]{:S(2)}) copy-start(bf16[8,128,128]{2,1,0:T(8,128)(2,1)} %param.7) | copy-start | bytes 786436
  7.9 0.7 copy-start.2
  10.2 7.4 %copy-start.3 = (s32[8,2]{0,1:T(2,128)S(1)}, s32[8,2]{0,1:T(2,128)}, u32[]{:S(2)}) copy-start(s32[8,2]{0,1:T(2,128)} %param.9) | copy-start | bytes 196
  10.2 13.8 %all-to-all-start = ((s32[8,1,2]{2,1,0:T(1,128)}), s32[8,1,2]{2,1,0:T(1,128)S(1)}, u32[]{:S(2)}, u32[]{:S(2)}) async-start(s32[8,1,2]{2,1,0:T(1,128)} %bitcast.7), calls=%async_computation | async-start | bytes 8192 | tf_op jit(solution)/shard_map/all_to_all | solution.py:34
  24.0 10.7 %all-to-all-start.2 = ((bf16[8,2,4096]{2,1,0:T(2,128)(2,1)}), bf16[8,2,4096]{2,1,0:T(2,128)(2,1)S(1)}, u32[]{:S(2)}, u32[]{:S(2)}) async-start(bf16[8,2,4096]{2,1,0:T(2,128)(2,1)} %reshape.80), calls=%async_computation.2 | async-start | bytes 262144 | tf_op jit(solution)/shard_map/all_to_all | solution.py:37
  34.6 10.7 %all-to-all-start.1 = ((bf16[8,2,4096]{2,1,0:T(2,128)(2,1)}), bf16[8,2,4096]{2,1,0:T(2,128)(2,1)S(1)}, u32[]{:S(2)}, u32[]{:S(2)}) async-start(bf16[8,2,4096]{2,1,0:T(2,128)(2,1)} %broadcast_select_fusion), calls=%async_computation.1 | async-start | bytes 262144 | tf_op jit(solution)/shard_map/all_to_all | solution.py:36
  38.0 44.8 %all-reduce.2.cloned.1.call-start = ((), (), s32[]{:S(2)}) async-start(), calls=%async_computation.3 | async-start | bytes 2097152 | tf_op jit(solution)/shard_map/psum | solution.py:58
  48.8 34.0 %copy-start.4 = (bf16[1024,256]{1,0:T(8,128)(2,1)S(1)}, bf16[1024,256]{1,0:T(8,128)(2,1)}, u32[]{:S(2)}) copy-start(bf16[1024,256]{1,0:T(8,128)(2,1)} %param.11) | copy-start | bytes 1572868
  82.8 39.5 %copy-start.1 = (f32[1024,256]{1,0:T(8,128)S(1)}, f32[1024,256]{1,0:T(8,128)}, u32[]{:S(2)}) copy-start(f32[1024,256]{1,0:T(8,128)} %all-reduce.2.cloned.1.call-done) | copy-start | bytes 3145732
Sparse Core Ops, SparseCore 0:
  48.9 33.8 all-reduce.1
where the time goes:
time: 131 us; the launch traced here: 130 us
  waiting for transfers between devices  48.4 us (37%)
  blocking collectives  37.7 us (29%)
  starting transfers between devices  14.2 us (11%)
  between operations  14.2 us (11%)
  local copies, waits for them, and re-layouts  7.28 us (6%)
  matrix products  4.85 us (4%)
  other arithmetic  3.66 us (3%)
    psum x1, blocking collectives, body(): grad_w = lax.psum(grad_part, 'row')  37.7 us
    psum x1, waiting for transfers between devices, body(): y_full = lax.psum(partial_y, 'col')  34 us
    all_to_all x1, starting transfers between devices, body(): lax.all_to_all(requests, 'row', split_axis=0, concat_axis=0, tiled=True)  7.41 us
    all_to_all x1, waiting for transfers between devices, body(): lax.all_to_all(picked, 'row', split_axis=0, concat_axis=0, tiled=True)  5.9 us
    all_to_all x1, waiting for transfers between devices, body(): lax.all_to_all(outgoing, 'row', split_axis=0, concat_axis=0, tiled=True)  5.33 us
    all_to_all x1, starting transfers between devices, body(): lax.all_to_all(picked, 'row', split_axis=0, concat_axis=0, tiled=True)  3.37 us
    all_to_all x1, starting transfers between devices, body(): lax.all_to_all(outgoing, 'row', split_axis=0, concat_axis=0, tiled=True)  3.37 us
    all_to_all x1, waiting for transfers between devices, body(): lax.all_to_all(requests, 'row', split_axis=0, concat_axis=0, tiled=True)  3.14 us
  transfers between devices with their start and end apart: 4, of which 4 were waited for; matrix products, arithmetic and copies ran while one was open for 5% of the time, Pallas kernels for 0%

commit v1 on v0

--- a/solution.py
+++ b/solution.py
@@ -2,6 +2,18 @@
 import jax.numpy as jnp
 from jax import lax
 from jax.sharding import PartitionSpec as P
+
+
+def in_blocks(value, dim, size):
+    shape = value.shape
+    blocks = value.reshape(*shape[:dim], size, shape[dim] // size, *shape[dim + 1 :])
+    return jnp.moveaxis(blocks, dim, 0)
+
+
+def laid_out(blocks, dim):
+    blocks = jnp.moveaxis(blocks, 0, dim)
+    shape = blocks.shape
+    return blocks.reshape(*shape[:dim], shape[dim] * shape[dim + 1], *shape[dim + 2 :])
 
 
 def body(x_t, tiles, tile_owner, tile_local, weight, cotangent):
@@ -31,7 +43,14 @@
         .set(mirror_terms.reshape(n_tiles, feat_q * tile_dim))
         .reshape(n_row, capacity, feat_q * tile_dim)
     )
-    block_ids = lax.all_to_all(requests, "row", split_axis=0, concat_axis=0, tiled=True)
+    size, here = (lax.axis_size("row"), lax.axis_index("row"))
+    pieces = in_blocks(requests, 0, size)
+    done = [pieces[here]]
+    for step in range(1, size):
+        sent = pieces[here ^ step]
+        done.append(lax.ppermute(sent, "row", [(i, i ^ step) for i in range(size)]))
+    pieces = jnp.stack(done)[here ^ jnp.arange(size)]
+    block_ids = laid_out(pieces, 0)
     picked = jnp.take(flat_blocks, block_ids, axis=0)
     fetched = lax.all_to_all(picked, "row", split_axis=0, concat_axis=0, tiled=True)
     incoming = lax.all_to_all(outgoing, "row", split_axis=0, concat_axis=0, tiled=True)

time: 131 us -> 133 us (1.015)
  starting transfers between devices: 14.2 us -> 23.7 us
  waiting for transfers between devices: 48.4 us -> 42.8 us
  other arithmetic: 3.66 us -> 2.25 us
    ppermute x0 -> x7, starting transfers between devices: none -> 14.9 us  [body(): done.append(lax.ppermute(sent, 'row', [(i, i ^ step) for i in range(size)]))]
    all_to_all x1 -> x0, starting transfers between devices: 7.41 us -> none  [body(): lax.all_to_all(requests, 'row', split_axis=0, concat_axis=0, tiled=True)]
    all_to_all x1, waiting for transfers between devices: 5.33 us -> 0.01 us  [body(): lax.all_to_all(outgoing, 'row', split_axis=0, concat_axis=0, tiled=True)]
    all_to_all x1 -> x0, waiting for transfers between devices: 3.14 us -> none  [body(): lax.all_to_all(requests, 'row', split_axis=0, concat_axis=0, tiled=True)]
    ppermute x0 -> x7, waiting for transfers between devices: none -> 1.62 us  [body(): done.append(lax.ppermute(sent, 'row', [(i, i ^ step) for i in range(size)]))]
  transfers between devices with their start and end apart: 4 -> 10, of which waited for: 4 -> 3; matrix products, arithmetic and copies ran while one was open for 5% -> 4% of each run, Pallas kernels for 0% -> 0%
where the time goes in v1:
time: 133 us; the launch traced here: 132 us
  waiting for transfers between devices  42.8 us (32%)
  blocking collectives  37.7 us (28%)
  starting transfers between devices  23.7 us (18%)
  between operations  14.3 us (11%)
  local copies, waits for them, and re-layouts  6.77 us (5%)
  matrix products  4.84 us (4%)
  other arithmetic  2.25 us (2%)
    psum x1, blocking collectives, body(): grad_w = lax.psum(grad_part, 'row')  37.7 us
    psum x1, waiting for transfers between devices, body(): y_full = lax.psum(partial_y, 'col')  34 us
    ppermute x7, starting transfers between devices, body(): done.append(lax.ppermute(sent, 'row', [(i, i ^ step) for i in range(size)]))  14.9 us
    all_to_all x1, waiting for transfers between devices, body(): lax.all_to_all(picked, 'row', split_axis=0, concat_axis=0, tiled=True)  7.14 us
    all_to_all x1, starting transfers between devices, body(): lax.all_to_all(picked, 'row', split_axis=0, concat_axis=0, tiled=True)  4.54 us
    all_to_all x1, starting transfers between devices, body(): lax.all_to_all(outgoing, 'row', split_axis=0, concat_axis=0, tiled=True)  4.2 us
  transfers between devices with their start and end apart: 10, of which 3 were waited for; matrix products, arithmetic and copies ran while one was open for 4% of the time, Pallas kernels for 0%

profile of v1, /device:TPU:0, one launch (start us, length us, event | category | flops | bytes accessed | tf_op | source)
XLA Modules:
  0.0 132.3 jit_solution(15235029811024995240)
XLA Ops:
  7.2 0.7 copy-done.4
  7.9 0.1 fusion.24
  8.0 0.2 select_reduce_fusion
  8.2 0.6 scatter_custom_fusion
  8.8 0.1 reshape_reshape.3
  8.9 6.1 %collective-permute-start.6 = (s32[1,2]{1,0:T(1,128)S(1)}, s32[1,2]{1,0:T(1,128)S(1)}, u32[]{:S(2)}, u32[]{:S(2)}) collective-permute-start(s32[1,2]{1,0:T(1,128)S(1)} %get-tuple-element.6), channel_id=1, source_target_pairs={{0,28},{4,24},{8,20},{12,16},{16,12},{20,8},{24,4},{28,0},{1,29},{... | collective-permute-start | bytes 32 | tf_op jit(solution)/shard_map/ppermute | solution.py:51
  15.0 0.2 collective-permute-start.5
  15.2 0.7 collective-permute-start.4
  15.9 2.0 %collective-permute-start.3 = (s32[1,2]{1,0:T(1,128)S(1)}, s32[1,2]{1,0:T(1,128)S(1)}, u32[]{:S(2)}, u32[]{:S(2)}) collective-permute-start(s32[1,2]{1,0:T(1,128)S(1)} %get-tuple-element.9), channel_id=1, source_target_pairs={{0,16},{4,20},{8,24},{12,28},{16,0},{20,4},{24,8},{28,12},{1,17},{... | collective-permute-start | bytes 32 | tf_op jit(solution)/shard_map/ppermute | solution.py:51
  18.0 2.3 %collective-permute-start.2 = (s32[1,2]{1,0:T(1,128)S(1)}, s32[1,2]{1,0:T(1,128)S(1)}, u32[]{:S(2)}, u32[]{:S(2)}) collective-permute-start(s32[1,2]{1,0:T(1,128)S(1)} %get-tuple-element.10), channel_id=1, source_target_pairs={{0,12},{4,8},{8,4},{12,0},{16,28},{20,24},{24,20},{28,16},{1,13},{... | collective-permute-start | bytes 32 | tf_op jit(solution)/shard_map/ppermute | solution.py:51
  20.3 0.6 gather_fusion.3
  20.9 0.2 fusion.1
  21.1 0.8 scatter_custom_fusion.1
  21.9 0.8 reshape.98
  22.7 4.2 %all-to-all-start.1 = ((bf16[8,2,4096]{2,1,0:T(2,128)(2,1)}), bf16[8,2,4096]{2,1,0:T(2,128)(2,1)S(1)}, u32[]{:S(2)}, u32[]{:S(2)}) async-start(bf16[8,2,4096]{2,1,0:T(2,128)(2,1)} %reshape.98), calls=%async_computation.1 | async-start | bytes 262144 | tf_op jit(solution)/shard_map/all_to_all | solution.py:56
  26.9 0.1 copy.59
  27.0 2.1 %collective-permute-start.1 = (s32[1,2]{1,0:T(1,128)S(1)}, s32[1,2]{1,0:T(1,128)S(1)}, u32[]{:S(2)}, u32[]{:S(2)}) collective-permute-start(s32[1,2]{1,0:T(1,128)S(1)} %get-tuple-element.11), channel_id=1, source_target_pairs={{0,8},{4,12},{8,0},{12,4},{16,24},{20,28},{24,16},{28,20},{1,9},{5... | collective-permute-start | bytes 32 | tf_op jit(solution)/shard_map/ppermute | solution.py:51
  29.1 0.1 copy.66
  29.2 1.5 %collective-permute-start = (s32[1,2]{1,0:T(1,128)S(1)}, s32[1,2]{1,0:T(1,128)S(1)}, u32[]{:S(2)}, u32[]{:S(2)}) collective-permute-start(s32[1,2]{1,0:T(1,128)S(1)} %get-tuple-element.12), channel_id=1, source_target_pairs={{0,4},{4,0},{8,12},{12,8},{16,20},{20,16},{24,28},{28,24},{1,5},{5... | collective-permute-start | bytes 32 | tf_op jit(solution)/shard_map/ppermute | solution.py:51
  30.7 0.1 copy.65
  30.8 0.1 copy.64
  30.8 0.1 copy.63
  30.9 0.1 copy.62
  31.0 0.1 copy.61
  31.1 1.6 %collective-permute-done = s32[1,2]{1,0:T(1,128)S(1)} collective-permute-done((s32[1,2]{1,0:T(1,128)S(1)}, s32[1,2]{1,0:T(1,128)S(1)}, u32[]{:S(2)}, u32[]{:S(2)}) %collective-permute-start) | collective-permute-done | bytes 40 | tf_op jit(solution)/shard_map/ppermute | solution.py:51
  32.7 0.1 copy.60
  32.8 0.1 stack.31
  32.9 0.1 copy.67
  33.0 0.6 gather_fusion
  33.6 0.1 copy.69
  33.7 0.1 copy.70
  33.8 0.1 reshape.112
  33.8 0.6 gather_fusion.1
  34.5 0.1 reshape.111
  34.6 0.8 broadcast_select_fusion
  35.4 4.5 %all-to-all-start = ((bf16[8,2,4096]{2,1,0:T(2,128)(2,1)}), bf16[8,2,4096]{2,1,0:T(2,128)(2,1)S(1)}, u32[]{:S(2)}, u32[]{:S(2)}) async-start(bf16[8,2,4096]{2,1,0:T(2,128)(2,1)} %broadcast_select_fusion), calls=%async_computation | async-start | bytes 262144 | tf_op jit(solution)/shard_map/all_to_all | solution.py:55
  40.0 0.1 eq.53
  40.2 7.1 %all-to-all-done = bf16[8,2,4096]{2,1,0:T(2,128)(2,1)S(1)} async-done(((bf16[8,2,4096]{2,1,0:T(2,128)(2,1)}), bf16[8,2,4096]{2,1,0:T(2,128)(2,1)S(1)}, u32[]{:S(2)}, u32[]{:S(2)}) %all-to-all-start) | async-done | bytes 131104 | tf_op jit(solution)/shard_map/all_to_all | solution.py:55
  47.3 0.1 reshape.96
  47.4 0.6 gather_fusion.2
  48.0 0.3 fusion.15
  48.3 0.3 fusion.5
  48.6 0.1 fusion
  48.7 2.1 %fusion.8 = f32[1024,256]{1,0:T(8,128)} fusion(bf16[4,8,8,128]{3,2,1,0:T(8,128)(2,1)S(1)} %bitcast.89, bf16[128,256]{1,0:T(8,128)(2,1)} %param.10, s32[]{:T(128)S(6)} %select_n.96), kind=kOutput, calls=%fused_computation.20 | convolution fusion | flops 16777216 | bytes 1130500 | tf_op jit(solution)/shard_map/dot_general | solution.py:74
  50.8 34.0 %all-reduce.2.cloned.1.call-done = f32[1024,256]{1,0:T(8,128)} async-done(((f32[1024,256]{1,0:T(8,128)}), f32[1024,256]{1,0:T(8,128)}) %all-reduce.2.cloned.1.call-update) | async-done | bytes 1048592 | tf_op jit(solution)/shard_map/psum | solution.py:77
  84.8 1.8 %fusion.2 = f32[32,256]{1,0:T(8,128)S(1)} fusion(f32[1024,256]{1,0:T(8,128)} %all-reduce.2.cloned.1.call-done, bf16[1024,256]{1,0:T(8,128)(2,1)S(1)} %copy-done.5, bf16[4,8,8,128]{3,2,1,0:T(8,128)(2,1)S(1)} %bitcast.90), kind=kOutput, calls=%fused_computation.13 | convolution fusion | flops 19398656 | bytes 1671168 | tf_op jit(solution)/shard_map/dot_general | solution.py:83
  86.7 37.7 %psum.15 = f32[32,256]{1,0:T(8,128)} all-reduce(f32[32,256]{1,0:T(8,128)S(1)} %fusion.2), channel_id=1, replica_groups=mesh['row'=8,'col'=4] {'row'}, use_global_device_ids=true, to_apply=%region_5.6 | all-reduce | flops 8192 | bytes 65536 | tf_op jit(solution)/shard_map/psum | solution.py:84
  124.3 1.1 multiply_convert_fusion.1
  (34 shorter events, 0.3 us)
Async XLA Ops:
  7.2 13.7 %copy-start = (bf16[8,128,128]{2,1,0:T(8,128)(2,1)S(1)}, bf16[8,128,128]{2,1,0:T(8,128)(2,1)}, u32[]{:S(2)}) copy-start(bf16[8,128,128]{2,1,0:T(8,128)(2,1)} %param.7) | copy-start | bytes 786436
  7.2 0.7 copy-start.4
  7.2 0.7 copy-start.3
  7.2 13.1 %copy-start.2 = (bf16[32,1024]{1,0:T(8,128)(2,1)S(1)}, bf16[32,1024]{1,0:T(8,128)(2,1)}, u32[]{:S(2)}) copy-start(bf16[32,1024]{1,0:T(8,128)(2,1)} %param.6) | copy-start | bytes 196612
  8.9 18.1 %collective-permute-start.6 = (s32[1,2]{1,0:T(1,128)S(1)}, s32[1,2]{1,0:T(1,128)S(1)}, u32[]{:S(2)}, u32[]{:S(2)}) collective-permute-start(s32[1,2]{1,0:T(1,128)S(1)} %get-tuple-element.6), channel_id=1, source_target_pairs={{0,28},{4,24},{8,20},{12,16},{16,12},{20,8},{24,4},{28,0},{1,29},{... | collective-permute-start | bytes 32 | tf_op jit(solution)/shard_map/ppermute | solution.py:51
  15.0 14.2 %collective-permute-start.5 = (s32[1,2]{1,0:T(1,128)S(1)}, s32[1,2]{1,0:T(1,128)S(1)}, u32[]{:S(2)}, u32[]{:S(2)}) collective-permute-start(s32[1,2]{1,0:T(1,128)S(1)} %get-tuple-element.7), channel_id=1, source_target_pairs={{0,24},{4,28},{8,16},{12,20},{16,8},{20,12},{24,0},{28,4},{1,25},{... | collective-permute-start | bytes 32 | tf_op jit(solution)/shard_map/ppermute | solution.py:51
  15.2 15.5 %collective-permute-start.4 = (s32[1,2]{1,0:T(1,128)S(1)}, s32[1,2]{1,0:T(1,128)S(1)}, u32[]{:S(2)}, u32[]{:S(2)}) collective-permute-start(s32[1,2]{1,0:T(1,128)S(1)} %get-tuple-element.8), channel_id=1, source_target_pairs={{0,20},{4,16},{8,28},{12,24},{16,4},{20,0},{24,12},{28,8},{1,21},{... | collective-permute-start | bytes 32 | tf_op jit(solution)/shard_map/ppermute | solution.py:51
  15.9 14.9 %collective-permute-start.3 = (s32[1,2]{1,0:T(1,128)S(1)}, s32[1,2]{1,0:T(1,128)S(1)}, u32[]{:S(2)}, u32[]{:S(2)}) collective-permute-start(s32[1,2]{1,0:T(1,128)S(1)} %get-tuple-element.9), channel_id=1, source_target_pairs={{0,16},{4,20},{8,24},{12,28},{16,0},{20,4},{24,8},{28,12},{1,17},{... | collective-permute-start | bytes 32 | tf_op jit(solution)/shard_map/ppermute | solution.py:51
  18.0 12.9 %collective-permute-start.2 = (s32[1,2]{1,0:T(1,128)S(1)}, s32[1,2]{1,0:T(1,128)S(1)}, u32[]{:S(2)}, u32[]{:S(2)}) collective-permute-start(s32[1,2]{1,0:T(1,128)S(1)} %get-tuple-element.10), channel_id=1, source_target_pairs={{0,12},{4,8},{8,4},{12,0},{16,28},{20,24},{24,20},{28,16},{1,13},{... | collective-permute-start | bytes 32 | tf_op jit(solution)/shard_map/ppermute | solution.py:51
  22.7 12.8 %all-to-all-start.1 = ((bf16[8,2,4096]{2,1,0:T(2,128)(2,1)}), bf16[8,2,4096]{2,1,0:T(2,128)(2,1)S(1)}, u32[]{:S(2)}, u32[]{:S(2)}) async-start(bf16[8,2,4096]{2,1,0:T(2,128)(2,1)} %reshape.98), calls=%async_computation.1 | async-start | bytes 262144 | tf_op jit(solution)/shard_map/all_to_all | solution.py:56
  27.0 4.0 %collective-permute-start.1 = (s32[1,2]{1,0:T(1,128)S(1)}, s32[1,2]{1,0:T(1,128)S(1)}, u32[]{:S(2)}, u32[]{:S(2)}) collective-permute-start(s32[1,2]{1,0:T(1,128)S(1)} %get-tuple-element.11), channel_id=1, source_target_pairs={{0,8},{4,12},{8,0},{12,4},{16,24},{20,28},{24,16},{28,20},{1,9},{5... | collective-permute-start | bytes 32 | tf_op jit(solution)/shard_map/ppermute | solution.py:51
  29.2 3.5 %collective-permute-start = (s32[1,2]{1,0:T(1,128)S(1)}, s32[1,2]{1,0:T(1,128)S(1)}, u32[]{:S(2)}, u32[]{:S(2)}) collective-permute-start(s32[1,2]{1,0:T(1,128)S(1)} %get-tuple-element.12), channel_id=1, source_target_pairs={{0,4},{4,0},{8,12},{12,8},{16,20},{20,16},{24,28},{28,24},{1,5},{5... | collective-permute-start | bytes 32 | tf_op jit(solution)/shard_map/ppermute | solution.py:51
  35.4 11.9 %all-to-all-start = ((bf16[8,2,4096]{2,1,0:T(2,128)(2,1)}), bf16[8,2,4096]{2,1,0:T(2,128)(2,1)S(1)}, u32[]{:S(2)}, u32[]{:S(2)}) async-start(bf16[8,2,4096]{2,1,0:T(2,128)(2,1)} %broadcast_select_fusion), calls=%async_computation | async-start | bytes 262144 | tf_op jit(solution)/shard_map/all_to_all | solution.py:55
  40.0 44.8 %all-reduce.2.cloned.1.call-start = ((), (), s32[]{:S(2)}) async-start(), calls=%async_computation.2 | async-start | bytes 2097152 | tf_op jit(solution)/shard_map/psum | solution.py:77
  50.8 34.0 %copy-start.5 = (bf16[1024,256]{1,0:T(8,128)(2,1)S(1)}, bf16[1024,256]{1,0:T(8,128)(2,1)}, u32[]{:S(2)}) copy-start(bf16[1024,256]{1,0:T(8,128)(2,1)} %param.11) | copy-start | bytes 1572868
  84.8 39.5 %copy-start.1 = (f32[1024,256]{1,0:T(8,128)S(1)}, f32[1024,256]{1,0:T(8,128)}, u32[]{:S(2)}) copy-start(f32[1024,256]{1,0:T(8,128)} %all-reduce.2.cloned.1.call-done) | copy-start | bytes 3145732
Sparse Core Ops, SparseCore 0:
  50.9 33.8 all-reduce.1
